TPU v7x, 128 devices: a whole 4x4x4 slice. The times are simulated.
128 devices in a mesh: seq: 32 (over x, y_hi, z), mp: 4 (over y_lo, core).
Axes of the slice: x: 4, y: 4 (y_hi: 2, y_lo: 2; y = y_hi * 2 + y_lo), z: 4, core: 2. Of those that a mesh axis runs over, the one named last changes fastest.
Arguments:
- hidden_in: bfloat16 [8192, 1536], P('seq', 'mp'), may hold values from -6 to 6
- wq: bfloat16 [1536, 1536], P('seq', 'mp'), may hold values from -1 to 1
- wkv: bfloat16 [1536, 512], P('seq'), may hold values from -0.15625 to 0.15625
- wo: bfloat16 [1536, 1536], P('mp', 'seq'), may hold values from -0.15625 to 0.15625
- lengths: int32 [3], replicated, may hold values from 1 to 6144, 8192 in all
- routes: int32 [8192, 4], P('seq'), may hold values from 0 to 31, all different within a row; in each aligned block of 256 rows (0 to 255, 256 to 511, ...) at most 64 rows name the same one
- gate_logits: float32 [8192, 4], P('seq'), may hold values from -6 to 6
- expert_gate: bfloat16 [32, 768, 1536], P('seq', 'mp'), may hold values from -0.15625 to 0.15625
- expert_up: bfloat16 [32, 768, 1536], P('seq', 'mp'), may hold values from -0.15625 to 0.15625
- expert_down: bfloat16 [32, 768, 1536], P('seq', 'mp'), may hold values from -0.21875 to 0.21875
Outputs:
- layer_out: bfloat16 [8192, 1536], P('seq', 'mp')
Inputs may be any that keep to these rules, and one draw needn't show every extreme that they name: `lengths`: sum to 8192; the longest is exactly 6144. `routes`: a token's 4 experts differ; among the rows of one device no expert is named more than 64 times, a bound that some block reaches.
All inputs are finite; a program needn't handle non-finite values.
Results may differ from a plain program's by a relative error of at most 0.018.
Values may be sent and summed in bfloat16 or wider, within the bound.
No kernel may reach another device: no remote copies, remote signals or barrier semaphores. Data moves between devices by JAX's collectives and lax.ppermute only.
A program may use at most 128 MiB of HBM per device.

v0:
```python
import math
import jax
import jax.numpy as jnp
from jax import lax
from jax.sharding import PartitionSpec as P

D = 1536
HQ = 12
KVH = 2
HD = 128
WINDOW = 4096
ROPE_BASE = 1500000.0
EPSILON = 1e-06


def prompt_ids(index, lengths):
    first_end = lengths[0]
    second_end = lengths[0] + lengths[1]
    prompt = (index >= first_end).astype(jnp.int32) + (index >= second_end).astype(jnp.int32)
    begin = jnp.where(index >= second_end, second_end, jnp.where(index >= first_end, first_end, 0))
    return (prompt, index - begin)


def rotary(values, position):
    half_dim = values.shape[-1] // 2
    freqs = jnp.exp(
        jnp.arange(half_dim, dtype=jnp.float32) * (-2.0 * math.log(ROPE_BASE) / values.shape[-1])
    )
    angles = position.astype(jnp.float32)[:, None] * freqs[None, :]
    cosine = jnp.cos(angles)[:, None, :]
    sine = jnp.sin(angles)[:, None, :]
    front = values[..., :half_dim]
    latter = values[..., half_dim:]
    return jnp.concatenate(
        [front * cosine - latter * sine, latter * cosine + front * sine], axis=-1
    )


def gather_seq(piece, count):
    rows = piece.shape[0]
    spread = jnp.broadcast_to(piece[None], (count,) + piece.shape).reshape(
        count * rows, piece.shape[1]
    )
    return lax.all_to_all(spread, "seq", 0, 0, tiled=True)


def local(
    hidden_in, wq, wkv, wo, lengths, routes, gate_logits, expert_gate, expert_up, expert_down
):
    tok_rows = hidden_in.shape[0]
    seq_index = lax.axis_index("seq")
    mp_index = lax.axis_index("mp")
    seq_count = lax.axis_size("seq")
    mp_count = lax.axis_size("mp")
    heads_here = wq.shape[1] // HD
    q_cols = heads_here * HD
    kv_group = mp_index * heads_here // (HQ // KVH)
    expert_all = lax.all_gather(
        jnp.concatenate([expert_gate, expert_up, expert_down], axis=0), "mp", axis=1, tiled=True
    )
    key_cols = lax.dynamic_slice_in_dim(wkv, kv_group * HD, HD, 1)
    value_cols = lax.dynamic_slice_in_dim(wkv, KVH * HD + kv_group * HD, HD, 1)
    piece = jnp.concatenate([wq, key_cols, value_cols, wo.T], axis=1)
    weights = gather_seq(piece, seq_count)
    w_qkv = weights[:, : q_cols + 2 * HD]
    wo_rows = weights[:, q_cols + 2 * HD :]
    whole = lax.all_gather(hidden_in, "mp", axis=1, tiled=True)
    whole_f = whole.astype(jnp.float32)
    normed = (
        whole_f * lax.rsqrt(jnp.sum(whole_f * whole_f, axis=-1, keepdims=True) / D + EPSILON)
    ).astype(jnp.bfloat16)
    lin = jnp.dot(normed, w_qkv, preferred_element_type=jnp.float32)
    own_index = seq_index * tok_rows + jnp.arange(tok_rows, dtype=jnp.int32)
    _, own_pos = prompt_ids(own_index, lengths)
    queries = (
        rotary(lin[:, :q_cols].reshape(tok_rows, heads_here, HD), own_pos)
        .astype(jnp.bfloat16)
        .transpose(1, 0, 2)
    )
    key_own = rotary(lin[:, q_cols : q_cols + HD].reshape(tok_rows, 1, HD), own_pos)[:, 0, :]
    value_own = lin[:, q_cols + HD :]
    kv_own = jnp.concatenate([key_own.astype(jnp.bfloat16), value_own.astype(jnp.bfloat16)], axis=1)
    back = min((WINDOW - 1 + tok_rows - 1) // tok_rows, seq_count - 1)
    blocks = []
    for k in range(back, 0, -1):
        blocks.append(lax.ppermute(kv_own, "seq", [(i, i + k) for i in range(seq_count - k)]))
    blocks.append(kv_own)
    kv_win = jnp.concatenate(blocks, axis=0)
    key_rows = kv_win[:, :HD]
    value_rows = kv_win[:, HD:].astype(jnp.float32)
    key_index = (seq_index - back) * tok_rows + jnp.arange((back + 1) * tok_rows, dtype=jnp.int32)
    scores = jnp.einsum(
        "hqd,kd->hqk", queries, key_rows, preferred_element_type=jnp.float32
    ) * HD ** (-0.5)
    query_prompt, _ = prompt_ids(own_index, lengths)
    key_prompt, _ = prompt_ids(key_index, lengths)
    spacing = own_index[:, None] - key_index[None, :]
    allowed = (
        (query_prompt[:, None] == key_prompt[None, :])
        & (spacing >= 0)
        & (spacing < WINDOW)
        & (key_index[None, :] >= 0)
    )[None]
    masked = jnp.where(allowed, scores, -1e30)
    peak = jnp.max(masked, axis=-1)
    probs = jnp.where(allowed, jnp.exp(masked - peak[..., None]), 0.0)
    total = jnp.sum(probs, axis=-1)
    accum = jnp.einsum("hqk,kd->hqd", probs, value_rows)
    attended = (
        (accum / total[..., None]).transpose(1, 0, 2).reshape(tok_rows, q_cols).astype(jnp.bfloat16)
    )
    partial_out = lax.dot_general(
        attended, wo_rows, (((1,), (1,)), ((), ())), preferred_element_type=jnp.float32
    )
    attn_mine = lax.psum_scatter(
        partial_out.astype(jnp.bfloat16), "mp", scatter_dimension=1, tiled=True
    ).astype(jnp.float32)
    residual = (hidden_in.astype(jnp.float32) + attn_mine).astype(jnp.bfloat16)
    residual_f = residual.astype(jnp.float32)
    square_sum = lax.psum(jnp.sum(residual_f * residual_f, axis=-1), "mp")
    moe_local = (residual_f * lax.rsqrt(square_sum / D + EPSILON)[:, None]).astype(jnp.bfloat16)
    local_experts = expert_gate.shape[0]
    experts = seq_count * local_experts
    top_count = routes.shape[1]
    capacity = 2 * tok_rows * top_count // experts
    part_cap = capacity // mp_count
    flat_ids = routes.reshape(-1)
    one_hot = (flat_ids[:, None] == jnp.arange(experts, dtype=jnp.int32)[None, :]).astype(jnp.int32)
    earlier_count = jnp.sum((jnp.cumsum(one_hot, axis=0) - one_hot) * one_hot, axis=1)
    mine = earlier_count // part_cap == mp_index
    slot_index = flat_ids * part_cap + earlier_count % part_cap
    send_index = jnp.where(mine, slot_index, experts * part_cap)
    source_row = jnp.arange(tok_rows * top_count, dtype=jnp.int32) // top_count
    full_rows = lax.all_gather(moe_local, "mp", axis=1, tiled=True)
    buffer = (
        jnp.zeros((experts * part_cap, D), jnp.bfloat16)
        .at[send_index]
        .set(full_rows[source_row], mode="drop")
    )
    arrived = lax.all_to_all(buffer, "seq", 0, 0, tiled=True)
    hidden_units = expert_all.shape[1]
    w_gate = expert_all[0]
    w_up = expert_all[1]
    w_down = expert_all[2]
    gate_act = lax.dot_general(
        arrived, w_gate, (((1,), (1,)), ((), ())), preferred_element_type=jnp.float32
    )
    up_act = lax.dot_general(
        arrived, w_up, (((1,), (1,)), ((), ())), preferred_element_type=jnp.float32
    )
    active = (jnp.maximum(gate_act, 0.0) * up_act).astype(jnp.bfloat16)
    result = jnp.dot(active, w_down, preferred_element_type=jnp.float32).astype(jnp.bfloat16)
    returned = lax.all_to_all(result, "seq", 0, 0, tiled=True)
    gate_weights = jax.nn.softmax(gate_logits, axis=-1)
    picked_back = returned[jnp.where(mine, slot_index, 0)].astype(jnp.float32)
    share = jnp.where(mine, gate_weights.reshape(-1), 0.0)
    weighted = picked_back * share[:, None]
    partial_moe = jnp.sum(weighted.reshape(tok_rows, top_count, D), axis=1)
    swapped = lax.all_to_all(partial_moe.astype(jnp.bfloat16), "mp", 1, 0, tiled=True)
    moe_total = jnp.sum(
        swapped.reshape(mp_count, tok_rows, D // mp_count).astype(jnp.float32), axis=0
    )
    del hidden_units
    return (residual_f + moe_total).astype(jnp.bfloat16)


def solution(mesh):
    return jax.shard_map(
        local,
        mesh=mesh,
        in_specs=(
            P("seq", "mp"),
            P("seq", "mp"),
            P("seq", None),
            P("mp", "seq"),
            P(),
            P("seq", None),
            P("seq", None),
            P("seq", "mp", None),
            P("seq", "mp", None),
            P("seq", "mp", None),
        ),
        out_specs=P("seq", "mp"),
        check_vma=False,
    )
```

profile of v0, /device:TPU:1, one launch (start us, length us, event | category | flops | bytes accessed | tf_op | source)
XLA Modules:
  0.0 351.0 jit_solution(2576738332656312989)
XLA Ops:
  8.1 2.0 broadcast_in_dim.38
  10.1 11.6 %all-to-all-start = ((bf16[32,48,1024]{2,1,0:T(8,128)(2,1)}), bf16[32,48,1024]{2,1,0:T(8,128)(2,1)}, u32[]{:S(2)}, u32[]{:S(2)}) async-start(bf16[32,48,1024]{2,1,0:T(8,128)(2,1)} %broadcast_in_dim.38), calls=%async_computation | async-start | bytes 6291456 | tf_op jit(solution)/shard_map/all_to_all | solution.py:44
  25.4 36.9 %all_gather.9 = bf16[256,1536]{1,0:T(8,128)(2,1)S(1)} all-gather(bf16[256,384]{1,0:T(8,128)(2,1)S(1)} %copy-done), channel_id=1, replica_groups=mesh['seq'=32,'mp'=4] {'mp'}, dimensions={1}, use_global_device_ids=true | all-gather | bytes 983040 | tf_op jit(solution)/shard_map/all_gather | solution.py:67
  64.7 2.4 fusion.15
  67.6 5.4 %collective-permute-start = (bf16[256,256]{0,1:T(8,128)(2,1)S(1)}, bf16[256,256]{0,1:T(8,128)(2,1)}, u32[]{:S(2)}, u32[]{:S(2)}) collective-permute-start(bf16[256,256]{0,1:T(8,128)(2,1)S(1)} %pad_maximum_fusion.1), channel_id=1, source_target_pairs={{0,64},{4,68},{8,72},{12,76},{16,80},{20,84},{24,88},{28,92},{32,9... | collective-permute-start | bytes 393224 | tf_op jit(solution)/shard_map/ppermute | solution.py:86
  73.0 10.4 %collective-permute-start.1 = (bf16[256,256]{0,1:T(8,128)(2,1)S(1)}, bf16[256,256]{0,1:T(8,128)(2,1)}, u32[]{:S(2)}, u32[]{:S(2)}) collective-permute-start(bf16[256,256]{0,1:T(8,128)(2,1)S(1)} %pad_maximum_fusion.1), channel_id=1, source_target_pairs={{0,60},{4,64},{8,68},{12,72},{16,76},{20,80},{24,84},{28,88},{32,9... | collective-permute-start | bytes 393224 | tf_op jit(solution)/shard_map/ppermute | solution.py:86
  83.5 2.7 collective-permute-start.2
  97.5 2.2 collective-permute-start.8
  100.6 5.7 %collective-permute-start.9 = (bf16[256,256]{0,1:T(8,128)(2,1)S(1)}, bf16[256,256]{0,1:T(8,128)(2,1)S(1)}, u32[]{:S(2)}, u32[]{:S(2)}) collective-permute-start(bf16[256,256]{0,1:T(8,128)(2,1)S(1)} %pad_maximum_fusion.1), channel_id=1, source_target_pairs={{0,28},{4,32},{8,36},{12,40},{16,44},{20,48},{24,52},{28,56},{32,6... | collective-permute-start | bytes 393224 | tf_op jit(solution)/shard_map/ppermute | solution.py:86
  108.6 4.0 %collective-permute-start.11 = (bf16[256,256]{0,1:T(8,128)(2,1)S(1)}, bf16[256,256]{0,1:T(8,128)(2,1)S(1)}, u32[]{:S(2)}, u32[]{:S(2)}) collective-permute-start(bf16[256,256]{0,1:T(8,128)(2,1)S(1)} %pad_maximum_fusion.1), channel_id=1, source_target_pairs={{0,20},{4,24},{8,28},{12,32},{16,36},{20,40},{24,44},{28,48},{32,5... | collective-permute-start | bytes 393224 | tf_op jit(solution)/shard_map/ppermute | solution.py:86
  113.9 4.6 %collective-permute-start.13 = (bf16[256,256]{0,1:T(8,128)(2,1)S(1)}, bf16[256,256]{0,1:T(8,128)(2,1)S(1)}, u32[]{:S(2)}, u32[]{:S(2)}) collective-permute-start(bf16[256,256]{0,1:T(8,128)(2,1)S(1)} %pad_maximum_fusion.1), channel_id=1, source_target_pairs={{0,12},{4,16},{8,20},{12,24},{16,28},{20,32},{24,36},{28,40},{32,4... | collective-permute-start | bytes 393224 | tf_op jit(solution)/shard_map/ppermute | solution.py:86
  120.3 3.8 %collective-permute-start.15 = (bf16[256,256]{0,1:T(8,128)(2,1)S(1)}, bf16[256,256]{0,1:T(8,128)(2,1)S(1)}, u32[]{:S(2)}, u32[]{:S(2)}) collective-permute-start(bf16[256,256]{0,1:T(8,128)(2,1)S(1)} %pad_maximum_fusion.1), channel_id=1, source_target_pairs={{0,4},{4,8},{8,12},{12,16},{16,20},{20,24},{24,28},{28,32},{32,36}... | collective-permute-start | bytes 393224 | tf_op jit(solution)/shard_map/ppermute | solution.py:86
  124.2 2.3 collective-permute-done.15
  126.5 6.4 %fusion = (f32[3,256]{1,0:T(4,128)S(1)}, f32[3,256,4352]{2,1,0:T(8,128)}) fusion(pred[256,4352]{1,0:T(8,128)(4,1)S(1)} %fusion.10, bf16[4352,256]{0,1:T(8,128)(2,1)S(1)} %constant_dynamic-update-slice_fusion, bf16[256,3,64]{2,0,1:T(8,128)(2,1)S(1)} %get-tuple-element.9, bf16[256,3,64]{2,0,1:T(8,128)(2,1)S(1)} %get-tuple-element.8), kind=kOutput, calls=%fused_computation.5 | convolution fusion | flops 866057472 | bytes 15993856 | tf_op jit(solution)/shard_map/hqd,kd->hqk/dot_general | solution.py:92
  132.9 9.0 %fusion.1 = f32[3,256]{1,0:T(4,128)S(1)} fusion(f32[3,256,4352]{2,1,0:T(8,128)} %get-tuple-element.21, f32[3,256]{1,0:T(4,128)S(1)} %get-tuple-element.20, pred[256,4352]{1,0:T(8,128)(4,1)S(1)} %fusion.10), kind=kLoop, calls=%fused_computation.6 | loop fusion | flops 16710912 | bytes 14489600 | tf_op jit(solution)/shard_map/reduce_sum | solution.py:107
  141.9 6.9 %fusion.23 = bf16[256,3,128]{0,2,1:T(8,128)(2,1)S(1)} fusion(bf16[4352,256]{0,1:T(8,128)(2,1)S(1)} %constant_dynamic-update-slice_fusion, f32[3,256,4352]{2,1,0:T(8,128)} %get-tuple-element.21, f32[3,256]{1,0:T(4,128)S(1)} %get-tuple-element.20, pred[256,4352]{1,0:T(8,128)(4,1)S(1)} %fusion.10, f32[256,3]{0,1:T(4,128)S(1)} %bitcast.93), kind=kOutput, calls=%fused_computation.43 | convolution fusion | flops 869203968 | bytes 15802368 | tf_op jit(solution)/shard_map/hqk,kd->hqd/dot_general | solution.py:108
  148.8 2.0 convolution_convert_fusion.1
  154.2 9.0 %reduce-window.6 = s32[32,8,128]{2,1,0:T(8,128)S(1)} reduce-window(s32[32,8,128]{2,1,0:T(8,128)S(1)} %fusion.36, s32[]{:T(128)} %constant.82.clone.1), window={size=1x1x128 pad=0_0x0_0x127_0}, to_apply=%region_4.5 | reduce-window | flops 4161536 | bytes 262148 | tf_op jit(solution)/shard_map/reduce-window
  164.0 11.4 %reduce-scatter.4.cloned.1.call-done = bf16[384,256]{1,0:T(8,128)(2,1)} async-done(((bf16[1536,256]{1,0:T(8,128)(2,1)}), bf16[384,256]{1,0:T(8,128)(2,1)}) %reduce-scatter.4.cloned.1.call-update) | async-done | bytes 196624
  176.7 5.1 %psum.7 = f32[256]{0:T(256)S(1)} all-reduce(f32[256]{0:T(256)S(1)} %fusion.28), channel_id=1, replica_groups=mesh['seq'=32,'mp'=4] {'mp'}, use_global_device_ids=true, to_apply=%region_8.9 | all-reduce | flops 256 | bytes 2048 | tf_op jit(solution)/shard_map/psum | solution.py:120
  181.9 9.9 %all_gather.10 = bf16[256,1536]{1,0:T(8,128)(2,1)S(1)} all-gather(bf16[256,384]{1,0:T(8,128)(2,1)S(1)} %fusion.29), channel_id=1, replica_groups=mesh['seq'=32,'mp'=4] {'mp'}, dimensions={1}, use_global_device_ids=true | all-gather | bytes 983040 | tf_op jit(solution)/shard_map/all_gather | solution.py:134
  191.8 16.3 %scatter_custom_fusion = bf16[512,1536]{1,0:T(8,128)(2,1)S(1)} fusion(s32[1024]{0:T(1024)S(1)} %bitcast.94, bf16[256,1536]{1,0:T(8,128)(2,1)S(1)} %all_gather.10, s32[1024]{0:T(1024)S(1)} %broadcast_clamp_fusion.1, bf16[]{:T(256)} %constant.99.clone.1), kind=kCustom, calls=%fused_computation.19 | custom fusion | bytes 1572866 | tf_op jit(solution)/shard_map/scatter | solution.py:138
  208.1 35.9 %all_to_all.43 = bf16[32,16,1536]{2,1,0:T(8,128)(2,1)S(1)} all-to-all(bf16[32,16,1536]{2,1,0:T(8,128)(2,1)S(1)} %bitcast.79), channel_id=1, replica_groups=mesh['seq'=32,'mp'=4] {'seq'}, dimensions={0} | all-to-all | bytes 3145728 | tf_op jit(solution)/shard_map/all_to_all | solution.py:140
  244.1 21.3 %all-gather.2.cloned.1.call-done = bf16[3,768,1536]{2,1,0:T(8,128)(2,1)} async-done(((bf16[3,192,1536]{2,1,0:T(8,128)(2,1)}), bf16[3,768,1536]{2,1,0:T(8,128)(2,1)}) %all-gather.2.cloned.1.call-update) | async-done | bytes 7077904 | tf_op jit(solution)/shard_map/all_gather | solution.py:58
  265.3 3.1 fusion.13
  268.4 6.7 %convolution_convert_fusion = bf16[512,1536]{1,0:T(8,128)(2,1)} fusion(bf16[3,768,1536]{2,1,0:T(8,128)(2,1)} %all-gather.2.cloned.1.call-done, f32[512,768]{1,0:T(8,128)S(1)} %fusion.13, bf16[512,1536]{1,0:T(8,128)(2,1)S(1)} %bitcast.83), kind=kOutput, calls=%fused_computation.21 | convolution fusion | flops 2417885184 | bytes 9437184 | tf_op jit(solution)/shard_map/dot_general | solution.py:152
  275.2 9.2 %all-to-all-start.2 = ((bf16[32,16,1536]{2,1,0:T(8,128)(2,1)}), bf16[32,16,1536]{2,1,0:T(8,128)(2,1)S(1)}, u32[]{:S(2)}, u32[]{:S(2)}) async-start(bf16[32,16,1536]{2,1,0:T(8,128)(2,1)} %bitcast.23), calls=%async_computation.2 | async-start | bytes 3145728 | tf_op jit(solution)/shard_map/all_to_all | solution.py:153
  284.9 24.1 %all-to-all-done.2 = bf16[32,16,1536]{2,1,0:T(8,128)(2,1)S(1)} async-done(((bf16[32,16,1536]{2,1,0:T(8,128)(2,1)}), bf16[32,16,1536]{2,1,0:T(8,128)(2,1)S(1)}, u32[]{:S(2)}, u32[]{:S(2)}) %all-to-all-start.2) | async-done | bytes 1572896 | tf_op jit(solution)/shard_map/all_to_all | solution.py:153
  309.0 5.6 %gather_fusion = bf16[1024,1536]{1,0:T(8,128)(2,1)} fusion(bf16[512,1536]{1,0:T(8,128)(2,1)S(1)} %bitcast.78, s32[1024]{0:T(1024)S(1)} %broadcast_clamp_fusion), kind=kCustom, calls=%fused_computation.1 | custom fusion | bytes 6295552 | tf_op jit(solution)/shard_map/gather | solution.py:155
  314.7 6.7 %reshape.440 = f32[256,4,1536]{2,1,0:T(4,128)} reshape(bf16[1024,1536]{1,0:T(8,128)(2,1)} %gather_fusion) | data formatting | bytes 9437184 | tf_op jit(solution)/shard_map/convert_element_type | solution.py:155
  321.3 7.4 %multiply_reduce_fusion = bf16[256,1536]{1,0:T(8,128)(2,1)S(1)} fusion(f32[256,4,1536]{2,1,0:T(4,128)} %reshape.440, f32[256,4]{1,0:T(8,128)S(1)} %copy.97), kind=kLoop, calls=%fused_computation.15 | loop fusion | flops 2752512 | bytes 7081984 | tf_op jit(solution)/shard_map/reduce_sum | solution.py:158
  329.4 13.7 %all_to_all.44 = bf16[256,4,384]{2,0,1:T(8,128)(2,1)S(1)} all-to-all(bf16[256,4,384]{2,0,1:T(8,128)(2,1)S(1)} %copy.99), channel_id=1, replica_groups=mesh['seq'=32,'mp'=4] {'mp'}, dimensions={1} | all-to-all | bytes 1572864 | tf_op jit(solution)/shard_map/all_to_all | solution.py:159
  (119 shorter events, 31.5 us)
Async XLA Ops:
  10.1 11.7 %copy-start.6 = (s32[3]{0:T(128)S(1)}, s32[3]{0:T(128)}, u32[]{:S(2)}) copy-start(s32[3]{0:T(128)} %param.14) | copy-start | bytes 40
  10.1 15.3 %copy-start = (bf16[256,384]{1,0:T(8,128)(2,1)S(1)}, bf16[256,384]{1,0:T(8,128)(2,1)}, u32[]{:S(2)}) copy-start(bf16[256,384]{1,0:T(8,128)(2,1)} %param.10) | copy-start | bytes 589828
  10.1 54.5 %all-to-all-start = ((bf16[32,48,1024]{2,1,0:T(8,128)(2,1)}), bf16[32,48,1024]{2,1,0:T(8,128)(2,1)}, u32[]{:S(2)}, u32[]{:S(2)}) async-start(bf16[32,48,1024]{2,1,0:T(8,128)(2,1)} %broadcast_in_dim.38), calls=%async_computation | async-start | bytes 6291456 | tf_op jit(solution)/shard_map/all_to_all | solution.py:44
  21.7 153.7 %reduce-scatter.4.cloned.1.call-start = ((), (), s32[]{:S(2)}) async-start(), calls=%async_computation.6 | async-start | bytes 983040
  67.6 23.1 %collective-permute-start = (bf16[256,256]{0,1:T(8,128)(2,1)S(1)}, bf16[256,256]{0,1:T(8,128)(2,1)}, u32[]{:S(2)}, u32[]{:S(2)}) collective-permute-start(bf16[256,256]{0,1:T(8,128)(2,1)S(1)} %pad_maximum_fusion.1), channel_id=1, source_target_pairs={{0,64},{4,68},{8,72},{12,76},{16,80},{20,84},{24,88},{28,92},{32,9... | collective-permute-start | bytes 393224 | tf_op jit(solution)/shard_map/ppermute | solution.py:86
  73.0 20.0 %collective-permute-start.1 = (bf16[256,256]{0,1:T(8,128)(2,1)S(1)}, bf16[256,256]{0,1:T(8,128)(2,1)}, u32[]{:S(2)}, u32[]{:S(2)}) collective-permute-start(bf16[256,256]{0,1:T(8,128)(2,1)S(1)} %pad_maximum_fusion.1), channel_id=1, source_target_pairs={{0,60},{4,64},{8,68},{12,72},{16,76},{20,80},{24,84},{28,88},{32,9... | collective-permute-start | bytes 393224 | tf_op jit(solution)/shard_map/ppermute | solution.py:86
  83.5 11.7 %collective-permute-start.2 = (bf16[256,256]{0,1:T(8,128)(2,1)S(1)}, bf16[256,256]{0,1:T(8,128)(2,1)}, u32[]{:S(2)}, u32[]{:S(2)}) collective-permute-start(bf16[256,256]{0,1:T(8,128)(2,1)S(1)} %pad_maximum_fusion.1), channel_id=1, source_target_pairs={{0,56},{4,60},{8,64},{12,68},{16,72},{20,76},{24,80},{28,84},{32,8... | collective-permute-start | bytes 393224 | tf_op jit(solution)/shard_map/ppermute | solution.py:86
  86.2 11.3 %collective-permute-start.3 = (bf16[256,256]{0,1:T(8,128)(2,1)S(1)}, bf16[256,256]{0,1:T(8,128)(2,1)}, u32[]{:S(2)}, u32[]{:S(2)}) collective-permute-start(bf16[256,256]{0,1:T(8,128)(2,1)S(1)} %pad_maximum_fusion.1), channel_id=1, source_target_pairs={{0,52},{4,56},{8,60},{12,64},{16,68},{20,72},{24,76},{28,80},{32,8... | collective-permute-start | bytes 393224 | tf_op jit(solution)/shard_map/ppermute | solution.py:86
  88.1 12.5 %collective-permute-start.4 = (bf16[256,256]{0,1:T(8,128)(2,1)S(1)}, bf16[256,256]{0,1:T(8,128)(2,1)}, u32[]{:S(2)}, u32[]{:S(2)}) collective-permute-start(bf16[256,256]{0,1:T(8,128)(2,1)S(1)} %pad_maximum_fusion.1), channel_id=1, source_target_pairs={{0,48},{4,52},{8,56},{12,60},{16,64},{20,68},{24,72},{28,76},{32,8... | collective-permute-start | bytes 393224 | tf_op jit(solution)/shard_map/ppermute | solution.py:86
  90.8 16.5 %collective-permute-start.5 = (bf16[256,256]{0,1:T(8,128)(2,1)S(1)}, bf16[256,256]{0,1:T(8,128)(2,1)S(1)}, u32[]{:S(2)}, u32[]{:S(2)}) collective-permute-start(bf16[256,256]{0,1:T(8,128)(2,1)S(1)} %pad_maximum_fusion.1), channel_id=1, source_target_pairs={{0,44},{4,48},{8,52},{12,56},{16,60},{20,64},{24,68},{28,72},{32,7... | collective-permute-start | bytes 393224 | tf_op jit(solution)/shard_map/ppermute | solution.py:86
  93.0 15.6 %collective-permute-start.6 = (bf16[256,256]{0,1:T(8,128)(2,1)S(1)}, bf16[256,256]{0,1:T(8,128)(2,1)S(1)}, u32[]{:S(2)}, u32[]{:S(2)}) collective-permute-start(bf16[256,256]{0,1:T(8,128)(2,1)S(1)} %pad_maximum_fusion.1), channel_id=1, source_target_pairs={{0,40},{4,44},{8,48},{12,52},{16,56},{20,60},{24,64},{28,68},{32,7... | collective-permute-start | bytes 393224 | tf_op jit(solution)/shard_map/ppermute | solution.py:86
  95.2 17.3 %collective-permute-start.7 = (bf16[256,256]{0,1:T(8,128)(2,1)S(1)}, bf16[256,256]{0,1:T(8,128)(2,1)S(1)}, u32[]{:S(2)}, u32[]{:S(2)}) collective-permute-start(bf16[256,256]{0,1:T(8,128)(2,1)S(1)} %pad_maximum_fusion.1), channel_id=1, source_target_pairs={{0,36},{4,40},{8,44},{12,48},{16,52},{20,56},{24,60},{28,64},{32,6... | collective-permute-start | bytes 393224 | tf_op jit(solution)/shard_map/ppermute | solution.py:86
  97.5 16.5 %collective-permute-start.8 = (bf16[256,256]{0,1:T(8,128)(2,1)S(1)}, bf16[256,256]{0,1:T(8,128)(2,1)S(1)}, u32[]{:S(2)}, u32[]{:S(2)}) collective-permute-start(bf16[256,256]{0,1:T(8,128)(2,1)S(1)} %pad_maximum_fusion.1), channel_id=1, source_target_pairs={{0,32},{4,36},{8,40},{12,44},{16,48},{20,52},{24,56},{28,60},{32,6... | collective-permute-start | bytes 393224 | tf_op jit(solution)/shard_map/ppermute | solution.py:86
  100.6 18.0 %collective-permute-start.9 = (bf16[256,256]{0,1:T(8,128)(2,1)S(1)}, bf16[256,256]{0,1:T(8,128)(2,1)S(1)}, u32[]{:S(2)}, u32[]{:S(2)}) collective-permute-start(bf16[256,256]{0,1:T(8,128)(2,1)S(1)} %pad_maximum_fusion.1), channel_id=1, source_target_pairs={{0,28},{4,32},{8,36},{12,40},{16,44},{20,48},{24,52},{28,56},{32,6... | collective-permute-start | bytes 393224 | tf_op jit(solution)/shard_map/ppermute | solution.py:86
  107.3 13.0 %collective-permute-start.10 = (bf16[256,256]{0,1:T(8,128)(2,1)S(1)}, bf16[256,256]{0,1:T(8,128)(2,1)S(1)}, u32[]{:S(2)}, u32[]{:S(2)}) collective-permute-start(bf16[256,256]{0,1:T(8,128)(2,1)S(1)} %pad_maximum_fusion.1), channel_id=1, source_target_pairs={{0,24},{4,28},{8,32},{12,36},{16,40},{20,44},{24,48},{28,52},{32,5... | collective-permute-start | bytes 393224 | tf_op jit(solution)/shard_map/ppermute | solution.py:86
  108.6 15.5 %collective-permute-start.11 = (bf16[256,256]{0,1:T(8,128)(2,1)S(1)}, bf16[256,256]{0,1:T(8,128)(2,1)S(1)}, u32[]{:S(2)}, u32[]{:S(2)}) collective-permute-start(bf16[256,256]{0,1:T(8,128)(2,1)S(1)} %pad_maximum_fusion.1), channel_id=1, source_target_pairs={{0,20},{4,24},{8,28},{12,32},{16,36},{20,40},{24,44},{28,48},{32,5... | collective-permute-start | bytes 393224 | tf_op jit(solution)/shard_map/ppermute | solution.py:86
  112.6 11.5 %collective-permute-start.12 = (bf16[256,256]{0,1:T(8,128)(2,1)S(1)}, bf16[256,256]{0,1:T(8,128)(2,1)S(1)}, u32[]{:S(2)}, u32[]{:S(2)}) collective-permute-start(bf16[256,256]{0,1:T(8,128)(2,1)S(1)} %pad_maximum_fusion.1), channel_id=1, source_target_pairs={{0,16},{4,20},{8,24},{12,28},{16,32},{20,36},{24,40},{28,44},{32,4... | collective-permute-start | bytes 393224 | tf_op jit(solution)/shard_map/ppermute | solution.py:86
  113.9 10.2 %collective-permute-start.13 = (bf16[256,256]{0,1:T(8,128)(2,1)S(1)}, bf16[256,256]{0,1:T(8,128)(2,1)S(1)}, u32[]{:S(2)}, u32[]{:S(2)}) collective-permute-start(bf16[256,256]{0,1:T(8,128)(2,1)S(1)} %pad_maximum_fusion.1), channel_id=1, source_target_pairs={{0,12},{4,16},{8,20},{12,24},{16,28},{20,32},{24,36},{28,40},{32,4... | collective-permute-start | bytes 393224 | tf_op jit(solution)/shard_map/ppermute | solution.py:86
  118.6 5.6 %collective-permute-start.14 = (bf16[256,256]{0,1:T(8,128)(2,1)S(1)}, bf16[256,256]{0,1:T(8,128)(2,1)S(1)}, u32[]{:S(2)}, u32[]{:S(2)}) collective-permute-start(bf16[256,256]{0,1:T(8,128)(2,1)S(1)} %pad_maximum_fusion.1), channel_id=1, source_target_pairs={{0,8},{4,12},{8,16},{12,20},{16,24},{20,28},{24,32},{28,36},{32,40... | collective-permute-start | bytes 393224 | tf_op jit(solution)/shard_map/ppermute | solution.py:86
  120.3 6.2 %collective-permute-start.15 = (bf16[256,256]{0,1:T(8,128)(2,1)S(1)}, bf16[256,256]{0,1:T(8,128)(2,1)S(1)}, u32[]{:S(2)}, u32[]{:S(2)}) collective-permute-start(bf16[256,256]{0,1:T(8,128)(2,1)S(1)} %pad_maximum_fusion.1), channel_id=1, source_target_pairs={{0,4},{4,8},{8,12},{12,16},{16,20},{20,24},{24,28},{28,32},{32,36}... | collective-permute-start | bytes 393224 | tf_op jit(solution)/shard_map/ppermute | solution.py:86
  148.8 3.4 copy-start.1
  148.8 3.4 copy-start.2
  148.8 3.4 copy-start.3
  152.1 1.6 copy-start.5
  152.2 113.2 %all-gather.2.cloned.1.call-start = ((), (), s32[]{:S(2)}) async-start(), calls=%async_computation.5 | async-start | bytes 8847360 | tf_op jit(solution)/shard_map/all_gather | solution.py:58
  275.2 9.5 %copy-start.4 = (f32[256,4]{0,1:T(4,128)S(1)}, f32[256,4]{0,1:T(4,128)}, u32[]{:S(2)}) copy-start(f32[256,4]{0,1:T(4,128)} %param.16) | copy-start | bytes 12292
  275.2 33.8 %all-to-all-start.2 = ((bf16[32,16,1536]{2,1,0:T(8,128)(2,1)}), bf16[32,16,1536]{2,1,0:T(8,128)(2,1)S(1)}, u32[]{:S(2)}, u32[]{:S(2)}) async-start(bf16[32,16,1536]{2,1,0:T(8,128)(2,1)} %bitcast.23), calls=%async_computation.2 | async-start | bytes 3145728 | tf_op jit(solution)/shard_map/all_to_all | solution.py:153
Sparse Core Ops, SparseCore 0:
  152.3 23.1 reduce-scatter.3
  177.1 88.1 all-gather.1
where the time goes:
time: 357 us; the launch traced here: 351 us
  blocking collectives  101 us (28%)
  starting transfers between devices  71.8 us (20%)
  waiting for transfers between devices  59.2 us (17%)
  local copies, waits for them, and re-layouts  41.8 us (12%)
  other arithmetic  33.7 us (9%)
  matrix products  27.5 us (8%)
  between operations  15.6 us (4%)
    ppermute x16, starting transfers between devices, local(): lax.ppermute(kv_own, 'seq', [(i, i + k) for i in range(seq_count - k)])  50.9 us
    all_gather x1, blocking collectives, local(): whole = lax.all_gather(hidden_in, 'mp', axis=1, tiled=True)  36.9 us
    all_to_all x1, blocking collectives, local(): arrived = lax.all_to_all(buffer, 'seq', 0, 0, tiled=True)  35.9 us
    all_to_all x1, waiting for transfers between devices, local(): returned = lax.all_to_all(result, 'seq', 0, 0, tiled=True)  24.1 us
    all_gather x1, waiting for transfers between devices, local(): lax.all_gather(jnp.concatenate([expert_gate, expert_up, expert_down], axi...  21.3 us
    scatter x1, local copies, waits for them, and re-layouts, local(): buffer = jnp.zeros((experts * part_cap, D), jnp.bfloat16).at[send_index]....  16.3 us
    all_to_all x1, blocking collectives, local(): lax.all_to_all(partial_moe.astype(jnp.bfloat16), 'mp', 1, 0, tiled=True)  13.7 us
    all_to_all x1, starting transfers between devices, gather_seq(): return lax.all_to_all(spread, 'seq', 0, 0, tiled=True)  11.6 us
  transfers between devices with their start and end apart: 20, of which 4 were waited for; matrix products, arithmetic and copies ran while one was open for 11% of the time, Pallas kernels for 0%

commit v1 on v0

--- a/solution.py
+++ b/solution.py
@@ -55,8 +55,17 @@
     heads_here = wq.shape[1] // HD
     q_cols = heads_here * HD
     kv_group = mp_index * heads_here // (HQ // KVH)
-    expert_all = lax.all_gather(
-        jnp.concatenate([expert_gate, expert_up, expert_down], axis=0), "mp", axis=1, tiled=True
+    expert_all = jnp.concatenate(
+        lax.all_to_all(
+            jnp.stack(
+                [jnp.concatenate([expert_gate, expert_up, expert_down], axis=0)]
+                * lax.axis_size("mp")
+            ),
+            "mp",
+            0,
+            0,
+        ),
+        axis=1,
     )
     key_cols = lax.dynamic_slice_in_dim(wkv, kv_group * HD, HD, 1)
     value_cols = lax.dynamic_slice_in_dim(wkv, KVH * HD + kv_group * HD, HD, 1)

time: 357 us -> 384 us (1.076)
  waiting for transfers between devices: 59.2 us -> 97.5 us
  blocking collectives: 101 us -> 66.8 us
  local copies, waits for them, and re-layouts: 41.8 us -> 52.7 us
  starting transfers between devices: 71.8 us -> 80.8 us
    all_to_all x1 -> x0, blocking collectives: 35.9 us -> none  [local(): arrived = lax.all_to_all(buffer, 'seq', 0, 0, tiled=True)]
    ppermute x16, waiting for transfers between devices: 2.31 us -> 30.7 us  [local(): lax.ppermute(kv_own, 'seq', [(i, i + k) for i in range(seq_count - k)])]
    all_gather x1 -> x0, waiting for transfers between devices: 21.3 us -> none  [local(): lax.all_gather(jnp.concatenate([expert_gate, expert_up, expert_down], axi...]
    unnamed x3 -> x2, waiting for transfers between devices: 11.4 us -> 29.1 us
    all_to_all x0 -> x2, waiting for transfers between devices: none -> 16.9 us  [the longest x1 16.9 us: local(): arrived = lax.all_to_all(buffer, 'seq', 0, 0, tiled=True)]
    all_to_all x0 -> x2, starting transfers between devices: none -> 14.9 us  [the longest x1 9.33 us: local(): arrived = lax.all_to_all(buffer, 'seq', 0, 0, tiled=True)]
    slice x2 -> x3, local copies, waits for them, and re-layouts: 0.22 us -> 6.32 us  [the longest x1 6.1 us: local(): w_up = expert_all[1]]
  transfers between devices with their start and end apart: 20 -> 21, of which waited for: 4 -> 7; matrix products, arithmetic and copies ran while one was open for 11% -> 20% of each run, Pallas kernels for 0% -> 0%
where the time goes in v1:
time: 384 us; the launch traced here: 377 us
  waiting for transfers between devices  97.5 us (25%)
  starting transfers between devices  80.8 us (21%)
  blocking collectives  66.8 us (17%)
  local copies, waits for them, and re-layouts  52.7 us (14%)
  other arithmetic  34 us (9%)
  matrix products  29 us (8%)
  between operations  15.6 us (4%)
    ppermute x16, starting transfers between devices, local(): lax.ppermute(kv_own, 'seq', [(i, i + k) for i in range(seq_count - k)])  48.8 us
    all_gather x1, blocking collectives, local(): whole = lax.all_gather(hidden_in, 'mp', axis=1, tiled=True)  36.2 us
    ppermute x16, waiting for transfers between devices, local(): lax.ppermute(kv_own, 'seq', [(i, i + k) for i in range(seq_count - k)])  30.7 us
    unnamed x2, waiting for transfers between devices  29.1 us
    all_to_all x1, waiting for transfers between devices, local(): returned = lax.all_to_all(result, 'seq', 0, 0, tiled=True)  20.9 us
    scatter x1, local copies, waits for them, and re-layouts, local(): buffer = jnp.zeros((experts * part_cap, D), jnp.bfloat16).at[send_index]....  17.2 us
    all_to_all x1, waiting for transfers between devices, local(): arrived = lax.all_to_all(buffer, 'seq', 0, 0, tiled=True)  16.9 us
    all_to_all x1, blocking collectives, local(): lax.all_to_all(partial_moe.astype(jnp.bfloat16), 'mp', 1, 0, tiled=True)  15.7 us
  transfers between devices with their start and end apart: 21, of which 7 were waited for; matrix products, arithmetic and copies ran while one was open for 20% of the time, Pallas kernels for 0%

profile of v1, /device:TPU:1, one launch (start us, length us, event | category | flops | bytes accessed | tf_op | source)
XLA Modules:
  0.0 376.5 jit_solution(5798769173820752925)
XLA Ops:
  10.1 11.6 %all-to-all-start = ((bf16[32,48,1024]{2,1,0:T(8,128)(2,1)}), bf16[32,48,1024]{2,1,0:T(8,128)(2,1)}, u32[]{:S(2)}, u32[]{:S(2)}) async-start(bf16[32,48,1024]{2,1,0:T(8,128)(2,1)} %broadcast_in_dim.38), calls=%async_computation | async-start | bytes 6291456 | tf_op jit(solution)/shard_map/all_to_all | solution.py:44
  26.1 36.2 %all_gather.6 = bf16[256,1536]{1,0:T(8,128)(2,1)S(1)} all-gather(bf16[256,384]{1,0:T(8,128)(2,1)S(1)} %copy-done.2), channel_id=1, replica_groups=mesh['seq'=32,'mp'=4] {'mp'}, dimensions={1}, use_global_device_ids=true | all-gather | bytes 983040 | tf_op jit(solution)/shard_map/all_gather | solution.py:76
  66.7 3.5 stack.2
  70.3 5.6 %all-to-all-start.2 = ((bf16[4,3,192,1536]{3,2,1,0:T(8,128)(2,1)}), bf16[4,3,192,1536]{3,2,1,0:T(8,128)(2,1)}, u32[]{:S(2)}, u32[]{:S(2)}) async-start(bf16[4,3,192,1536]{3,2,1,0:T(8,128)(2,1)} %stack.2), calls=%async_computation.2 | async-start | bytes 14155776 | tf_op jit(solution)/shard_map/all_to_all | solution.py:59
  78.9 5.4 %collective-permute-start = (bf16[256,256]{0,1:T(8,128)(2,1)S(1)}, bf16[256,256]{0,1:T(8,128)(2,1)}, u32[]{:S(2)}, u32[]{:S(2)}) collective-permute-start(bf16[256,256]{0,1:T(8,128)(2,1)S(1)} %pad_maximum_fusion.1), channel_id=1, source_target_pairs={{0,64},{4,68},{8,72},{12,76},{16,80},{20,84},{24,88},{28,92},{32,9... | collective-permute-start | bytes 393224 | tf_op jit(solution)/shard_map/ppermute | solution.py:95
  84.3 10.5 %collective-permute-start.1 = (bf16[256,256]{0,1:T(8,128)(2,1)S(1)}, bf16[256,256]{0,1:T(8,128)(2,1)}, u32[]{:S(2)}, u32[]{:S(2)}) collective-permute-start(bf16[256,256]{0,1:T(8,128)(2,1)S(1)} %pad_maximum_fusion.1), channel_id=1, source_target_pairs={{0,60},{4,64},{8,68},{12,72},{16,76},{20,80},{24,84},{28,88},{32,9... | collective-permute-start | bytes 393224 | tf_op jit(solution)/shard_map/ppermute | solution.py:95
  94.7 2.7 collective-permute-start.2
  108.7 2.4 collective-permute-start.8
  112.1 5.5 %collective-permute-start.9 = (bf16[256,256]{0,1:T(8,128)(2,1)S(1)}, bf16[256,256]{0,1:T(8,128)(2,1)S(1)}, u32[]{:S(2)}, u32[]{:S(2)}) collective-permute-start(bf16[256,256]{0,1:T(8,128)(2,1)S(1)} %pad_maximum_fusion.1), channel_id=1, source_target_pairs={{0,28},{4,32},{8,36},{12,40},{16,44},{20,48},{24,52},{28,56},{32,6... | collective-permute-start | bytes 393224 | tf_op jit(solution)/shard_map/ppermute | solution.py:95
  119.8 4.2 %collective-permute-start.11 = (bf16[256,256]{0,1:T(8,128)(2,1)S(1)}, bf16[256,256]{0,1:T(8,128)(2,1)S(1)}, u32[]{:S(2)}, u32[]{:S(2)}) collective-permute-start(bf16[256,256]{0,1:T(8,128)(2,1)S(1)} %pad_maximum_fusion.1), channel_id=1, source_target_pairs={{0,20},{4,24},{8,28},{12,32},{16,36},{20,40},{24,44},{28,48},{32,5... | collective-permute-start | bytes 393224 | tf_op jit(solution)/shard_map/ppermute | solution.py:95
  125.5 4.6 %collective-permute-start.13 = (bf16[256,256]{0,1:T(8,128)(2,1)S(1)}, bf16[256,256]{0,1:T(8,128)(2,1)S(1)}, u32[]{:S(2)}, u32[]{:S(2)}) collective-permute-start(bf16[256,256]{0,1:T(8,128)(2,1)S(1)} %pad_maximum_fusion.1), channel_id=1, source_target_pairs={{0,12},{4,16},{8,20},{12,24},{16,28},{20,32},{24,36},{28,40},{32,4... | collective-permute-start | bytes 393224 | tf_op jit(solution)/shard_map/ppermute | solution.py:95
  130.1 24.9 %collective-permute-done.9 = bf16[256,256]{0,1:T(8,128)(2,1)S(1)} collective-permute-done((bf16[256,256]{0,1:T(8,128)(2,1)S(1)}, bf16[256,256]{0,1:T(8,128)(2,1)S(1)}, u32[]{:S(2)}, u32[]{:S(2)}) %collective-permute-start.9) | collective-permute-done | bytes 131104 | tf_op jit(solution)/shard_map/ppermute | solution.py:95
  161.1 2.8 collective-permute-done.12
  164.0 6.4 %fusion = (f32[3,256]{1,0:T(4,128)S(1)}, f32[3,256,4352]{2,1,0:T(8,128)}) fusion(pred[256,4352]{1,0:T(8,128)(4,1)S(1)} %fusion.10, bf16[4352,256]{0,1:T(8,128)(2,1)S(1)} %constant_dynamic-update-slice_fusion, bf16[256,3,64]{2,0,1:T(8,128)(2,1)S(1)} %get-tuple-element.12, bf16[256,3,64]{2,0,1:T(8,128)(2,1)S(1)} %get-tuple-element.11), kind=kOutput, calls=%fused_computation.5 | convolution fusion | flops 866057472 | bytes 15993856 | tf_op jit(solution)/shard_map/hqd,kd->hqk/dot_general | solution.py:101
  170.4 9.0 %fusion.1 = f32[3,256]{1,0:T(4,128)S(1)} fusion(f32[3,256,4352]{2,1,0:T(8,128)} %get-tuple-element.24, f32[3,256]{1,0:T(4,128)S(1)} %get-tuple-element.23, pred[256,4352]{1,0:T(8,128)(4,1)S(1)} %fusion.10), kind=kLoop, calls=%fused_computation.6 | loop fusion | flops 16710912 | bytes 14489600 | tf_op jit(solution)/shard_map/reduce_sum | solution.py:116
  179.4 6.9 %fusion.21 = bf16[256,3,128]{0,2,1:T(8,128)(2,1)S(1)} fusion(bf16[4352,256]{0,1:T(8,128)(2,1)S(1)} %constant_dynamic-update-slice_fusion, f32[3,256,4352]{2,1,0:T(8,128)} %get-tuple-element.24, f32[3,256]{1,0:T(4,128)S(1)} %get-tuple-element.23, pred[256,4352]{1,0:T(8,128)(4,1)S(1)} %fusion.10, f32[256,3]{0,1:T(4,128)S(1)} %bitcast.90), kind=kOutput, calls=%fused_computation.38 | convolution fusion | flops 869203968 | bytes 15802368 | tf_op jit(solution)/shard_map/hqk,kd->hqd/dot_general | solution.py:117
  189.4 9.0 %reduce-window.6 = s32[32,8,128]{2,1,0:T(8,128)S(1)} reduce-window(s32[32,8,128]{2,1,0:T(8,128)S(1)} %fusion.33, s32[]{:T(128)} %constant.82.clone.1), window={size=1x1x128 pad=0_0x0_0x127_0}, to_apply=%region_4.5 | reduce-window | flops 4161536 | bytes 262148 | tf_op jit(solution)/shard_map/reduce-window
  199.3 29.1 %reduce-scatter.4.cloned.1.call-done = bf16[384,256]{1,0:T(8,128)(2,1)} async-done(((bf16[1536,256]{1,0:T(8,128)(2,1)}), bf16[384,256]{1,0:T(8,128)(2,1)}) %reduce-scatter.4.cloned.1.call-update) | async-done | bytes 196624
  229.6 5.3 %psum.7 = f32[256]{0:T(256)S(1)} all-reduce(f32[256]{0:T(256)S(1)} %fusion.25), channel_id=1, replica_groups=mesh['seq'=32,'mp'=4] {'mp'}, use_global_device_ids=true, to_apply=%region_8.9 | all-reduce | flops 256 | bytes 2048 | tf_op jit(solution)/shard_map/psum | solution.py:129
  235.1 9.6 %all_gather.7 = bf16[256,1536]{1,0:T(8,128)(2,1)S(1)} all-gather(bf16[256,384]{1,0:T(8,128)(2,1)S(1)} %fusion.26), channel_id=1, replica_groups=mesh['seq'=32,'mp'=4] {'mp'}, dimensions={1}, use_global_device_ids=true | all-gather | bytes 983040 | tf_op jit(solution)/shard_map/all_gather | solution.py:143
  244.7 17.2 %scatter_custom_fusion = bf16[512,1536]{1,0:T(8,128)(2,1)} fusion(s32[1024]{0:T(1024)S(1)} %bitcast.91, bf16[256,1536]{1,0:T(8,128)(2,1)S(1)} %all_gather.7, s32[1024]{0:T(1024)S(1)} %broadcast_clamp_fusion.1, bf16[]{:T(256)} %constant.99.clone.1), kind=kCustom, calls=%fused_computation.19 | custom fusion | bytes 1572866 | tf_op jit(solution)/shard_map/scatter | solution.py:147
  261.9 9.3 %all-to-all-start.1 = ((bf16[32,16,1536]{2,1,0:T(8,128)(2,1)}), bf16[32,16,1536]{2,1,0:T(8,128)(2,1)S(1)}, u32[]{:S(2)}, u32[]{:S(2)}) async-start(bf16[32,16,1536]{2,1,0:T(8,128)(2,1)} %bitcast.18), calls=%async_computation.1 | async-start | bytes 3145728 | tf_op jit(solution)/shard_map/all_to_all | solution.py:149
  271.2 6.1 %fusion.58 = (bf16[1,4,192,1536]{3,2,0,1:T(8,128)(2,1)}, bf16[1,4,192,1536]{3,2,0,1:T(8,128)(2,1)}, bf16[1,4,192,1536]{3,2,0,1:T(8,128)(2,1)}) fusion(bf16[3,4,192,1536]{3,2,0,1:T(8,128)(2,1)} %bitcast.20), kind=kLoop, calls=%fused_computation.142 | loop fusion | bytes 14155776 | tf_op jit(solution)/shard_map/slice | solution.py:152
  277.3 16.9 %all-to-all-done.1 = bf16[32,16,1536]{2,1,0:T(8,128)(2,1)S(1)} async-done(((bf16[32,16,1536]{2,1,0:T(8,128)(2,1)}), bf16[32,16,1536]{2,1,0:T(8,128)(2,1)S(1)}, u32[]{:S(2)}, u32[]{:S(2)}) %all-to-all-start.1) | async-done | bytes 1572896 | tf_op jit(solution)/shard_map/all_to_all | solution.py:149
  294.2 4.3 %fusion.61 = f32[512,768]{1,0:T(8,128)} fusion(bf16[512,1536]{1,0:T(8,128)(2,1)S(1)} %bitcast.79, bf16[768,1536]{1,0:T(8,128)(2,1)} %bitcast.77), kind=kOutput, calls=%fused_computation.145 | convolution fusion | flops 1207959552 | bytes 5505024 | tf_op jit(solution)/shard_map/dot_general | solution.py:154
  298.5 7.2 %convolution_convert_fusion = bf16[512,1536]{1,0:T(8,128)(2,1)} fusion(bf16[768,1536]{1,0:T(8,128)(2,1)} %bitcast.76, f32[512,768]{1,0:T(8,128)} %fusion.61, bf16[512,1536]{1,0:T(8,128)(2,1)S(1)} %bitcast.80, bf16[768,1536]{1,0:T(8,128)(2,1)} %bitcast.75), kind=kOutput, calls=%fused_computation.21 | convolution fusion | flops 2417885184 | bytes 9437184 | tf_op jit(solution)/shard_map/dot_general | solution.py:161
  305.7 5.5 %all-to-all-start.3 = ((bf16[32,16,1536]{2,1,0:T(8,128)(2,1)}), bf16[32,16,1536]{2,1,0:T(8,128)(2,1)S(1)}, u32[]{:S(2)}, u32[]{:S(2)}) async-start(bf16[32,16,1536]{2,1,0:T(8,128)(2,1)} %bitcast.78), calls=%async_computation.3 | async-start | bytes 3145728 | tf_op jit(solution)/shard_map/all_to_all | solution.py:162
  311.7 20.9 %all-to-all-done.3 = bf16[32,16,1536]{2,1,0:T(8,128)(2,1)S(1)} async-done(((bf16[32,16,1536]{2,1,0:T(8,128)(2,1)}), bf16[32,16,1536]{2,1,0:T(8,128)(2,1)S(1)}, u32[]{:S(2)}, u32[]{:S(2)}) %all-to-all-start.3) | async-done | bytes 1572896 | tf_op jit(solution)/shard_map/all_to_all | solution.py:162
  332.5 5.6 %gather_fusion = bf16[1024,1536]{1,0:T(8,128)(2,1)} fusion(bf16[512,1536]{1,0:T(8,128)(2,1)S(1)} %bitcast.72, s32[1024]{0:T(1024)S(1)} %broadcast_clamp_fusion), kind=kCustom, calls=%fused_computation.1 | custom fusion | bytes 6295552 | tf_op jit(solution)/shard_map/gather | solution.py:164
  338.1 6.7 %reshape.453 = f32[256,4,1536]{2,1,0:T(4,128)} reshape(bf16[1024,1536]{1,0:T(8,128)(2,1)} %gather_fusion) | data formatting | bytes 9437184 | tf_op jit(solution)/shard_map/convert_element_type | solution.py:164
  344.8 7.4 %multiply_reduce_fusion = bf16[256,1536]{1,0:T(8,128)(2,1)S(1)} fusion(f32[256,4,1536]{2,1,0:T(4,128)} %reshape.453, f32[256,4]{1,0:T(8,128)S(1)} %copy.97), kind=kLoop, calls=%fused_computation.15 | loop fusion | flops 2752512 | bytes 7081984 | tf_op jit(solution)/shard_map/reduce_sum | solution.py:167
  352.9 15.7 %all_to_all.48 = bf16[256,4,384]{2,0,1:T(8,128)(2,1)S(1)} all-to-all(bf16[256,4,384]{2,0,1:T(8,128)(2,1)S(1)} %copy.99), channel_id=1, replica_groups=mesh['seq'=32,'mp'=4] {'mp'}, dimensions={1} | all-to-all | bytes 1572864 | tf_op jit(solution)/shard_map/all_to_all | solution.py:168
  (121 shorter events, 42.8 us)
Async XLA Ops:
  10.1 11.6 %copy-start.5 = (s32[256,4]{0,1:T(4,128)S(1)}, s32[256,4]{0,1:T(4,128)}, u32[]{:S(2)}) copy-start(s32[256,4]{0,1:T(4,128)} %param.15) | copy-start | bytes 12292
  10.1 12.0 %copy-start.6 = (s32[3]{0:T(128)S(1)}, s32[3]{0:T(128)}, u32[]{:S(2)}) copy-start(s32[3]{0:T(128)} %param.14) | copy-start | bytes 40
  10.1 16.0 %copy-start.2 = (bf16[256,384]{1,0:T(8,128)(2,1)S(1)}, bf16[256,384]{1,0:T(8,128)(2,1)}, u32[]{:S(2)}) copy-start(bf16[256,384]{1,0:T(8,128)(2,1)} %param.10) | copy-start | bytes 589828
  10.1 56.6 %all-to-all-start = ((bf16[32,48,1024]{2,1,0:T(8,128)(2,1)}), bf16[32,48,1024]{2,1,0:T(8,128)(2,1)}, u32[]{:S(2)}, u32[]{:S(2)}) async-start(bf16[32,48,1024]{2,1,0:T(8,128)(2,1)} %broadcast_in_dim.38), calls=%async_computation | async-start | bytes 6291456 | tf_op jit(solution)/shard_map/all_to_all | solution.py:44
  21.7 42.0 %copy-start.3 = (bf16[1,192,1536]{2,1,0:T(8,128)(2,1)S(1)}, bf16[1,192,1536]{2,1,0:T(8,128)(2,1)}, u32[]{:S(2)}) copy-start(bf16[1,192,1536]{2,1,0:T(8,128)(2,1)} %param.19) | copy-start | bytes 1769476
  62.3 0.9 copy-start
  70.2 5.6 %copy-start.1 = (bf16[256,1536]{1,0:T(8,128)(2,1)S(1)}, bf16[256,1536]{1,0:T(8,128)(2,1)}, u32[]{:S(2)}) copy-start(bf16[256,1536]{1,0:T(8,128)(2,1)} %copy-done) | copy-start | bytes 2359300
  70.3 191.6 %all-to-all-start.2 = ((bf16[4,3,192,1536]{3,2,1,0:T(8,128)(2,1)}), bf16[4,3,192,1536]{3,2,1,0:T(8,128)(2,1)}, u32[]{:S(2)}, u32[]{:S(2)}) async-start(bf16[4,3,192,1536]{3,2,1,0:T(8,128)(2,1)} %stack.2), calls=%async_computation.2 | async-start | bytes 14155776 | tf_op jit(solution)/shard_map/all_to_all | solution.py:59
  75.9 152.5 %reduce-scatter.4.cloned.1.call-start = ((), (), s32[]{:S(2)}) async-start(), calls=%async_computation.6 | async-start | bytes 983040
  78.9 23.1 %collective-permute-start = (bf16[256,256]{0,1:T(8,128)(2,1)S(1)}, bf16[256,256]{0,1:T(8,128)(2,1)}, u32[]{:S(2)}, u32[]{:S(2)}) collective-permute-start(bf16[256,256]{0,1:T(8,128)(2,1)S(1)} %pad_maximum_fusion.1), channel_id=1, source_target_pairs={{0,64},{4,68},{8,72},{12,76},{16,80},{20,84},{24,88},{28,92},{32,9... | collective-permute-start | bytes 393224 | tf_op jit(solution)/shard_map/ppermute | solution.py:95
  84.3 20.0 %collective-permute-start.1 = (bf16[256,256]{0,1:T(8,128)(2,1)S(1)}, bf16[256,256]{0,1:T(8,128)(2,1)}, u32[]{:S(2)}, u32[]{:S(2)}) collective-permute-start(bf16[256,256]{0,1:T(8,128)(2,1)S(1)} %pad_maximum_fusion.1), channel_id=1, source_target_pairs={{0,60},{4,64},{8,68},{12,72},{16,76},{20,80},{24,84},{28,88},{32,9... | collective-permute-start | bytes 393224 | tf_op jit(solution)/shard_map/ppermute | solution.py:95
  94.7 11.7 %collective-permute-start.2 = (bf16[256,256]{0,1:T(8,128)(2,1)S(1)}, bf16[256,256]{0,1:T(8,128)(2,1)}, u32[]{:S(2)}, u32[]{:S(2)}) collective-permute-start(bf16[256,256]{0,1:T(8,128)(2,1)S(1)} %pad_maximum_fusion.1), channel_id=1, source_target_pairs={{0,56},{4,60},{8,64},{12,68},{16,72},{20,76},{24,80},{28,84},{32,8... | collective-permute-start | bytes 393224 | tf_op jit(solution)/shard_map/ppermute | solution.py:95
  97.4 11.3 %collective-permute-start.3 = (bf16[256,256]{0,1:T(8,128)(2,1)S(1)}, bf16[256,256]{0,1:T(8,128)(2,1)}, u32[]{:S(2)}, u32[]{:S(2)}) collective-permute-start(bf16[256,256]{0,1:T(8,128)(2,1)S(1)} %pad_maximum_fusion.1), channel_id=1, source_target_pairs={{0,52},{4,56},{8,60},{12,64},{16,68},{20,72},{24,76},{28,80},{32,8... | collective-permute-start | bytes 393224 | tf_op jit(solution)/shard_map/ppermute | solution.py:95
  99.4 12.7 %collective-permute-start.4 = (bf16[256,256]{0,1:T(8,128)(2,1)S(1)}, bf16[256,256]{0,1:T(8,128)(2,1)}, u32[]{:S(2)}, u32[]{:S(2)}) collective-permute-start(bf16[256,256]{0,1:T(8,128)(2,1)S(1)} %pad_maximum_fusion.1), channel_id=1, source_target_pairs={{0,48},{4,52},{8,56},{12,60},{16,64},{20,68},{24,72},{28,76},{32,8... | collective-permute-start | bytes 393224 | tf_op jit(solution)/shard_map/ppermute | solution.py:95
  102.0 16.5 %collective-permute-start.5 = (bf16[256,256]{0,1:T(8,128)(2,1)S(1)}, bf16[256,256]{0,1:T(8,128)(2,1)S(1)}, u32[]{:S(2)}, u32[]{:S(2)}) collective-permute-start(bf16[256,256]{0,1:T(8,128)(2,1)S(1)} %pad_maximum_fusion.1), channel_id=1, source_target_pairs={{0,44},{4,48},{8,52},{12,56},{16,60},{20,64},{24,68},{28,72},{32,7... | collective-permute-start | bytes 393224 | tf_op jit(solution)/shard_map/ppermute | solution.py:95
  104.3 15.6 %collective-permute-start.6 = (bf16[256,256]{0,1:T(8,128)(2,1)S(1)}, bf16[256,256]{0,1:T(8,128)(2,1)S(1)}, u32[]{:S(2)}, u32[]{:S(2)}) collective-permute-start(bf16[256,256]{0,1:T(8,128)(2,1)S(1)} %pad_maximum_fusion.1), channel_id=1, source_target_pairs={{0,40},{4,44},{8,48},{12,52},{16,56},{20,60},{24,64},{28,68},{32,7... | collective-permute-start | bytes 393224 | tf_op jit(solution)/shard_map/ppermute | solution.py:95
  106.5 17.6 %collective-permute-start.7 = (bf16[256,256]{0,1:T(8,128)(2,1)S(1)}, bf16[256,256]{0,1:T(8,128)(2,1)S(1)}, u32[]{:S(2)}, u32[]{:S(2)}) collective-permute-start(bf16[256,256]{0,1:T(8,128)(2,1)S(1)} %pad_maximum_fusion.1), channel_id=1, source_target_pairs={{0,36},{4,40},{8,44},{12,48},{16,52},{20,56},{24,60},{28,64},{32,6... | collective-permute-start | bytes 393224 | tf_op jit(solution)/shard_map/ppermute | solution.py:95
  108.7 16.7 %collective-permute-start.8 = (bf16[256,256]{0,1:T(8,128)(2,1)S(1)}, bf16[256,256]{0,1:T(8,128)(2,1)S(1)}, u32[]{:S(2)}, u32[]{:S(2)}) collective-permute-start(bf16[256,256]{0,1:T(8,128)(2,1)S(1)} %pad_maximum_fusion.1), channel_id=1, source_target_pairs={{0,32},{4,36},{8,40},{12,44},{16,48},{20,52},{24,56},{28,60},{32,6... | collective-permute-start | bytes 393224 | tf_op jit(solution)/shard_map/ppermute | solution.py:95
  112.1 42.9 %collective-permute-start.9 = (bf16[256,256]{0,1:T(8,128)(2,1)S(1)}, bf16[256,256]{0,1:T(8,128)(2,1)S(1)}, u32[]{:S(2)}, u32[]{:S(2)}) collective-permute-start(bf16[256,256]{0,1:T(8,128)(2,1)S(1)} %pad_maximum_fusion.1), channel_id=1, source_target_pairs={{0,28},{4,32},{8,36},{12,40},{16,44},{20,48},{24,52},{28,56},{32,6... | collective-permute-start | bytes 393224 | tf_op jit(solution)/shard_map/ppermute | solution.py:95
  118.5 39.3 %collective-permute-start.10 = (bf16[256,256]{0,1:T(8,128)(2,1)S(1)}, bf16[256,256]{0,1:T(8,128)(2,1)S(1)}, u32[]{:S(2)}, u32[]{:S(2)}) collective-permute-start(bf16[256,256]{0,1:T(8,128)(2,1)S(1)} %pad_maximum_fusion.1), channel_id=1, source_target_pairs={{0,24},{4,28},{8,32},{12,36},{16,40},{20,44},{24,48},{28,52},{32,5... | collective-permute-start | bytes 393224 | tf_op jit(solution)/shard_map/ppermute | solution.py:95
  119.8 41.2 %collective-permute-start.11 = (bf16[256,256]{0,1:T(8,128)(2,1)S(1)}, bf16[256,256]{0,1:T(8,128)(2,1)S(1)}, u32[]{:S(2)}, u32[]{:S(2)}) collective-permute-start(bf16[256,256]{0,1:T(8,128)(2,1)S(1)} %pad_maximum_fusion.1), channel_id=1, source_target_pairs={{0,20},{4,24},{8,28},{12,32},{16,36},{20,40},{24,44},{28,48},{32,5... | collective-permute-start | bytes 393224 | tf_op jit(solution)/shard_map/ppermute | solution.py:95
  124.1 39.7 %collective-permute-start.12 = (bf16[256,256]{0,1:T(8,128)(2,1)S(1)}, bf16[256,256]{0,1:T(8,128)(2,1)S(1)}, u32[]{:S(2)}, u32[]{:S(2)}) collective-permute-start(bf16[256,256]{0,1:T(8,128)(2,1)S(1)} %pad_maximum_fusion.1), channel_id=1, source_target_pairs={{0,16},{4,20},{8,24},{12,28},{16,32},{20,36},{24,40},{28,44},{32,4... | collective-permute-start | bytes 393224 | tf_op jit(solution)/shard_map/ppermute | solution.py:95
  125.5 38.4 %collective-permute-start.13 = (bf16[256,256]{0,1:T(8,128)(2,1)S(1)}, bf16[256,256]{0,1:T(8,128)(2,1)S(1)}, u32[]{:S(2)}, u32[]{:S(2)}) collective-permute-start(bf16[256,256]{0,1:T(8,128)(2,1)S(1)} %pad_maximum_fusion.1), channel_id=1, source_target_pairs={{0,12},{4,16},{8,20},{12,24},{16,28},{20,32},{24,36},{28,40},{32,4... | collective-permute-start | bytes 393224 | tf_op jit(solution)/shard_map/ppermute | solution.py:95
  155.0 8.9 %collective-permute-start.14 = (bf16[256,256]{0,1:T(8,128)(2,1)S(1)}, bf16[256,256]{0,1:T(8,128)(2,1)S(1)}, u32[]{:S(2)}, u32[]{:S(2)}) collective-permute-start(bf16[256,256]{0,1:T(8,128)(2,1)S(1)} %pad_maximum_fusion.1), channel_id=1, source_target_pairs={{0,8},{4,12},{8,16},{12,20},{16,24},{20,28},{24,32},{28,36},{32,40... | collective-permute-start | bytes 393224 | tf_op jit(solution)/shard_map/ppermute | solution.py:95
  157.8 6.1 %collective-permute-start.15 = (bf16[256,256]{0,1:T(8,128)(2,1)S(1)}, bf16[256,256]{0,1:T(8,128)(2,1)S(1)}, u32[]{:S(2)}, u32[]{:S(2)}) collective-permute-start(bf16[256,256]{0,1:T(8,128)(2,1)S(1)} %pad_maximum_fusion.1), channel_id=1, source_target_pairs={{0,4},{4,8},{8,12},{12,16},{16,20},{20,24},{24,28},{28,32},{32,36}... | collective-permute-start | bytes 393224 | tf_op jit(solution)/shard_map/ppermute | solution.py:95
  261.9 32.3 %all-to-all-start.1 = ((bf16[32,16,1536]{2,1,0:T(8,128)(2,1)}), bf16[32,16,1536]{2,1,0:T(8,128)(2,1)S(1)}, u32[]{:S(2)}, u32[]{:S(2)}) async-start(bf16[32,16,1536]{2,1,0:T(8,128)(2,1)} %bitcast.18), calls=%async_computation.1 | async-start | bytes 3145728 | tf_op jit(solution)/shard_map/all_to_all | solution.py:149
  305.7 5.7 %copy-start.4 = (f32[256,4]{0,1:T(4,128)S(1)}, f32[256,4]{0,1:T(4,128)}, u32[]{:S(2)}) copy-start(f32[256,4]{0,1:T(4,128)} %param.16) | copy-start | bytes 12292
  305.7 26.8 %all-to-all-start.3 = ((bf16[32,16,1536]{2,1,0:T(8,128)(2,1)}), bf16[32,16,1536]{2,1,0:T(8,128)(2,1)S(1)}, u32[]{:S(2)}, u32[]{:S(2)}) async-start(bf16[32,16,1536]{2,1,0:T(8,128)(2,1)} %bitcast.78), calls=%async_computation.3 | async-start | bytes 3145728 | tf_op jit(solution)/shard_map/all_to_all | solution.py:162
Sparse Core Ops, SparseCore 0:
  189.5 38.8 reduce-scatter.3
